TPU v7x, 256 devices: a whole 4x4x8 slice. The times are simulated.
256 devices in a mesh: ctx: 32 (over y, z), head: 8 (over x, core).
Axes of the slice: x: 4, y: 4, z: 8, core: 2. Of those that a mesh axis runs over, the one named last changes fastest.
Arguments:
- queries: bfloat16 [4096, 4096], P('ctx', 'head'), may hold values from -30 to 30
- key_proj: bfloat16 [4096, 1024], P('ctx', 'head'), may hold values from -6 to 6
- value_proj: bfloat16 [4096, 1024], P('ctx', 'head'), may hold values from -6 to 6
- lengths: int32 [32], replicated, may hold values from 1 to 2048, 4096 in all
- out_weight: bfloat16 [4096, 8192], P(None, 'head'), may hold values from -0.09375 to 0.09375
Outputs:
- mixed_out: bfloat16 [4096, 8192], P('ctx', 'head')
Inputs may be any that keep to these rules, and one draw needn't show every extreme that they name: Document lengths in pack order; they sum to 4096 and the longest is exactly 2048.
All inputs are finite; a program needn't handle non-finite values.
Results may differ from a plain program's by a relative error of at most 0.005.
The roundings to bfloat16 on the way count: a program that leaves them out, or rounds other values in their place, can miss the bound.
Values may be sent and summed in bfloat16 or wider, within the bound.
No kernel may reach another device: no remote copies, remote signals or barrier semaphores. Data moves between devices by JAX's collectives and lax.ppermute only.
A program may use at most 64 MiB of HBM per device.

v0:
```python
import jax
import jax.numpy as jnp
from jax import lax
from jax.sharding import PartitionSpec as P

HD = 128
rope_theta = 500000.0


def doc_starts(lengths, positions):
    doc_ends = jnp.cumsum(lengths)
    picked = jnp.where(doc_ends[None, :] <= positions[:, None], lengths[None, :], 0)
    return jnp.sum(picked, axis=1)


def rotary(projected, offsets, head_dim):
    token_count = projected.shape[0]
    heads_grid = projected.astype(jnp.float32).reshape(token_count, -1, head_dim)
    half_dim = head_dim // 2
    inverse = rope_theta ** (-2.0 * jnp.arange(half_dim).astype(jnp.float32) / head_dim)
    angles = offsets.astype(jnp.float32)[:, None] * inverse[None, :]
    cosine = jnp.cos(angles)[:, None, :]
    sine_part = jnp.sin(angles)[:, None, :]
    first_half = heads_grid[..., :half_dim]
    second_half = heads_grid[..., half_dim:]
    rotated = jnp.concatenate(
        [
            first_half * cosine - second_half * sine_part,
            second_half * cosine + first_half * sine_part,
        ],
        axis=-1,
    )
    return rotated.reshape(token_count, -1).astype(jnp.bfloat16)


def on_device(queries, key_proj, value_proj, lengths, out_weight):
    tok_rows = queries.shape[0]
    kv_local = key_proj.shape[1] // HD
    query_group = queries.shape[1] // key_proj.shape[1]
    first_row = lax.axis_index("ctx") * tok_rows
    positions = first_row + jnp.arange(tok_rows, dtype=jnp.int32)
    starts = doc_starts(lengths, positions)
    offsets = positions - starts
    q_rot = rotary(queries, offsets, HD).reshape(tok_rows, kv_local, query_group, HD)
    k_rot = rotary(key_proj, offsets, HD)
    lowest = starts[0]
    initial = (
        jnp.full((kv_local, query_group, tok_rows), -1e30, jnp.float32),
        jnp.zeros((kv_local, query_group, tok_rows), jnp.float32),
        jnp.zeros((kv_local, query_group, tok_rows, HD), jnp.float32),
    )
    begin_row = jnp.int32(0)
    key_part = lax.all_gather(k_rot, "ctx", axis=0, tiled=True)
    value_part = lax.all_gather(value_proj, "ctx", axis=0, tiled=True)
    key_count = key_part.shape[0]

    def update(state):
        running_max, running_sum, weighted = state
        key_block = key_part.reshape(key_count, kv_local, HD)
        value_block = value_part.reshape(key_count, kv_local, HD)
        scores = jnp.einsum(
            "tkgd,nkd->kgtn", q_rot, key_block, preferred_element_type=jnp.float32
        ) / jnp.sqrt(jnp.float32(HD))
        key_pos = jnp.arange(key_count, dtype=jnp.int32)
        allowed = (key_pos[None, :] <= positions[:, None]) & (key_pos[None, :] >= starts[:, None])
        scores = jnp.where(allowed, scores, -1e30)
        new_max = jnp.maximum(running_max, jnp.max(scores, axis=-1))
        weights = jnp.where(allowed, jnp.exp(scores - new_max[..., None]), 0.0)
        new_sum = jnp.sum(weights, axis=-1)
        product = jnp.einsum(
            "kgtn,nkd->kgtd",
            weights.astype(jnp.bfloat16),
            value_block,
            preferred_element_type=jnp.float32,
        )
        return (new_max, new_sum, product)

    needed = (begin_row <= first_row + tok_rows - 1) & (begin_row + key_count - 1 >= lowest)
    state = lax.cond(needed, update, lambda state: state, initial)
    running_max, running_sum, weighted = state
    normed = (weighted / running_sum[..., None]).astype(jnp.bfloat16)
    attended = jnp.transpose(normed, (2, 0, 1, 3)).reshape(tok_rows, kv_local * query_group * HD)
    mixed_out = jnp.dot(
        lax.all_gather(attended, "head", axis=1, tiled=True),
        out_weight,
        preferred_element_type=jnp.float32,
    )
    return mixed_out.astype(jnp.bfloat16)


def solution(mesh):
    placed = (P("ctx", "head"), P("ctx", "head"), P("ctx", "head"), P(), P(None, "head"))
    return jax.shard_map(
        on_device, mesh=mesh, in_specs=placed, out_specs=P("ctx", "head"), check_vma=False
    )
```

profile of v0, /device:TPU:1, one launch (start us, length us, event | category | flops | bytes accessed | tf_op | source)
XLA Modules:
  0.0 206.3 jit_solution(5268036091979652018)
XLA Ops:
  6.5 0.0 all-gather.5.cloned.1.call-start
  6.5 0.7 all-gather.5.cloned.1.call-update
  7.3 0.0 all-gather.9.cloned.1.call-start
  7.3 0.7 copy.19
  8.0 0.1 reduce-window.8
  8.1 0.1 reduce.2
  8.2 0.9 copy.21
  9.1 0.7 select_reduce_fusion
  9.9 0.2 fusion.23
  10.1 0.6 pad_maximum_fusion.1
  10.7 0.0 all-gather.9.cloned.1.call-update
  10.7 0.0 all-gather.7.cloned.1.call-start
  10.8 1.0 copy.20
  11.9 0.2 multiply_cosine_fusion.1
  12.2 72.9 %all-gather.5.cloned.1.call-done = bf16[4096,128]{1,0:T(8,128)(2,1)} async-done(((bf16[128,128]{1,0:T(8,128)(2,1)}), bf16[4096,128]{1,0:T(8,128)(2,1)}) %all-gather.5.cloned.1.call-update) | async-done | bytes 1048592 | tf_op jit(solution)/shard_map/all_gather | solution.py:54
  85.0 71.6 %all-gather.9.cloned.1.call-done = bf16[4096,1,128]{0,2,1:T(8,128)(2,1)} async-done(((bf16[128,1,128]{0,2,1:T(8,128)(2,1)}), bf16[4096,1,128]{0,2,1:T(8,128)(2,1)}) %all-gather.9.cloned.1.call-update) | async-done | bytes 1048592 | tf_op jit(solution)/shard_map/all_gather | solution.py:53
  156.6 7.3 %conditional.1 = (f32[1,4,128]{2,1,0:T(4,128)S(1)}, f32[1,4,128,128]{2,3,1,0:T(8,128)S(1)}) conditional(s32[]{:T(128)} %convert_element_type.42, () %tuple.13, (s32[]{:T(128)}, s32[128]{0:T(128)S(1)}, s32[128]{0:T(128)S(1)}, bf16[128,4,128]{0,2,1:T(8,128)(2,1)S(1)}, bf16[4096,128]{0,1:T(8,128)(2,1)}, /*index=5*/bf16[4096,128]{1,0:T(8,128)(2,1)}) %tuple.32), branch_computations={%region_2.3_spmd, %region_3.6_spmd} | conditional | flops 1102577280 | bytes 34224176 | solution.py:79
  156.6 0.0 copy-start
  156.6 0.1 copy.22
  156.8 0.5 fusion.7
  157.3 2.6 %fusion = (f32[4,128]{1,0:T(4,128)S(1)}, f32[4096,128,4]{1,0,2:T(8,128)S(1)}) fusion(pred[128,4096]{0,1:T(8,128)(4,1)S(1)} %fusion.7, bf16[128,4,128]{2,0,1:T(8,128)(2,1)S(1)} %copy.22, bf16[4096,128]{0,1:T(8,128)(2,1)} %get-tuple-element.47), kind=kOutput, calls=%fused_computation.2 | convolution fusion | flops 543161856 | bytes 10094592 | tf_op jit(solution)/shard_map/cond/branch_1_fun/tkgd,nkd->kgtn/dot_general | solution.py:61
  159.8 0.0 copy-done
  159.9 2.0 fusion.8
  161.8 2.1 %fusion.2 = f32[4,128]{1,0:T(4,128)S(1)} fusion(f32[4096,128,4]{1,0,2:T(8,128)S(1)} %get-tuple-element.51, f32[4,128]{1,0:T(4,128)S(1)} %broadcast_maximum_fusion, pred[128,4096]{0,1:T(8,128)(4,1)S(1)} %fusion.7), kind=kLoop, calls=%fused_computation.4 | loop fusion | flops 10485248 | bytes 8916992 | tf_op jit(solution)/shard_map/cond/branch_1_fun/reduce_sum | solution.py:69
  163.9 0.7 divide_convert_fusion
  164.6 0.0 all-gather.7.cloned.1.call-update
  164.6 29.4 %all-gather.7.cloned.1.call-done = bf16[128,4096]{0,1:T(8,128)(2,1)} async-done(((bf16[128,512]{0,1:T(8,128)(2,1)}), bf16[128,4096]{0,1:T(8,128)(2,1)}) %all-gather.7.cloned.1.call-update) | async-done | bytes 1048592 | tf_op jit(solution)/shard_map/all_gather | solution.py:84
  194.1 5.7 %convolution_convert_fusion = bf16[128,1024]{1,0:T(8,128)(2,1)} fusion(bf16[128,4096]{0,1:T(8,128)(2,1)} %all-gather.7.cloned.1.call-done, bf16[4096,1024]{1,0:T(8,128)(2,1)} %param.11), kind=kOutput, calls=%fused_computation.21 | convolution fusion | flops 1073872896 | bytes 9699328 | tf_op jit(solution)/shard_map/dot_general | solution.py:83
  (10 shorter events, 0.1 us)
Async XLA Ops:
  6.5 78.5 %all-gather.5.cloned.1.call-start = ((), (), s32[]{:S(2)}) async-start(), calls=%async_computation | async-start | bytes 1081344 | tf_op jit(solution)/shard_map/all_gather | solution.py:54
  7.3 149.4 %all-gather.9.cloned.1.call-start = ((), (), s32[]{:S(2)}) async-start(), calls=%async_computation.2 | async-start | bytes 1081344 | tf_op jit(solution)/shard_map/all_gather | solution.py:53
  10.7 183.3 %all-gather.7.cloned.1.call-start = ((), (), s32[]{:S(2)}) async-start(), calls=%async_computation.1 | async-start | bytes 1179648 | tf_op jit(solution)/shard_map/all_gather | solution.py:84
  156.6 3.2 %copy-start = (bf16[4096,128]{1,0:T(8,128)(2,1)S(1)}, bf16[4096,128]{1,0:T(8,128)(2,1)}, u32[]{:S(2)}) copy-start(bf16[4096,128]{1,0:T(8,128)(2,1)} %get-tuple-element.26) | copy-start | bytes 3145732 | tf_op jit(solution)/shard_map/cond
Sparse Core Ops, SparseCore 0:
  9.9 75.0 all-gather.4
  87.5 69.0 all-gather.8
  164.8 29.2 all-gather.6
where the time goes:
time: 207 us; the launch traced here: 206 us
  waiting for transfers between devices  175 us (85%)
  between operations  13.2 us (6%)
  matrix products  10.3 us (5%)
  other arithmetic  5.29 us (3%)
  local copies, waits for them, and re-layouts  2.76 us (1%)
    all_gather x1, waiting for transfers between devices, on_device(): value_part = lax.all_gather(value_proj, 'ctx', axis=0, tiled=True)  72.9 us
    all_gather x1, waiting for transfers between devices, on_device(): key_part = lax.all_gather(k_rot, 'ctx', axis=0, tiled=True)  71.6 us
    all_gather x1, waiting for transfers between devices, on_device(): lax.all_gather(attended, 'head', axis=1, tiled=True)  29.4 us
    dot_general x1, matrix products, on_device(): jnp.dot(lax.all_gather(attended, 'head', axis=1, tiled=True), out_weight,...  5.7 us
  transfers between devices with their start and end apart: 3, of which 3 were waited for; matrix products, arithmetic and copies ran while one was open for 2% of the time, Pallas kernels for 0%

commit v1 on v0

--- a/solution.py
+++ b/solution.py
@@ -51,7 +51,9 @@
     )
     begin_row = jnp.int32(0)
     key_part = lax.all_gather(k_rot, "ctx", axis=0, tiled=True)
-    value_part = lax.all_gather(value_proj, "ctx", axis=0, tiled=True)
+    value_part = jnp.concatenate(
+        lax.all_to_all(jnp.stack([value_proj] * lax.axis_size("ctx")), "ctx", 0, 0), axis=0
+    )
     key_count = key_part.shape[0]
 
     def update(state):

time: 207 us -> 134 us (0.65)
  waiting for transfers between devices: 175 us -> 87.4 us
  starting transfers between devices: 0.08 us -> 12.1 us
    all_gather x1 -> x0, waiting for transfers between devices: 72.9 us -> none  [on_device(): value_part = lax.all_gather(value_proj, 'ctx', axis=0, tiled=True)]
    all_gather x1, waiting for transfers between devices: 71.6 us -> 57.9 us  [on_device(): key_part = lax.all_gather(k_rot, 'ctx', axis=0, tiled=True)]
    all_to_all x0 -> x1, starting transfers between devices: none -> 12 us  [on_device(): lax.all_to_all(jnp.stack([value_proj] * lax.axis_size('ctx')), 'ctx', 0, 0)]
  transfers between devices with their start and end apart: 3 -> 3, of which waited for: 3 -> 2; matrix products, arithmetic and copies ran while one was open for 2% -> 2% of each run, Pallas kernels for 0% -> 0%
where the time goes in v1:
time: 134 us; the launch traced here: 133 us
  waiting for transfers between devices  87.4 us (65%)
  between operations  13.5 us (10%)
  starting transfers between devices  12.1 us (9%)
  matrix products  10.2 us (8%)
  other arithmetic  5.29 us (4%)
  local copies, waits for them, and re-layouts  4.79 us (4%)
    all_gather x1, waiting for transfers between devices, on_device(): key_part = lax.all_gather(k_rot, 'ctx', axis=0, tiled=True)  57.9 us
    all_gather x1, waiting for transfers between devices, on_device(): lax.all_gather(attended, 'head', axis=1, tiled=True)  29.4 us
    all_to_all x1, starting transfers between devices, on_device(): lax.all_to_all(jnp.stack([value_proj] * lax.axis_size('ctx')), 'ctx', 0, 0)  12 us
    dot_general x1, matrix products, on_device(): jnp.dot(lax.all_gather(attended, 'head', axis=1, tiled=True), out_weight,...  5.7 us
  transfers between devices with their start and end apart: 3, of which 2 were waited for; matrix products, arithmetic and copies ran while one was open for 2% of the time, Pallas kernels for 0%

profile of v1, /device:TPU:1, one launch (start us, length us, event | category | flops | bytes accessed | tf_op | source)
XLA Modules:
  0.0 133.3 jit_solution(1358570965065763114)
XLA Ops:
  6.5 0.0 all-gather.6.cloned.1.call-start
  6.5 0.7 copy.19
  7.3 0.1 reduce-window.8
  7.3 0.1 reduce.2
  7.5 0.7 select_reduce_fusion
  8.2 0.9 copy.21
  9.1 0.2 fusion.22
  9.3 0.6 pad_maximum_fusion.1
  9.9 0.0 all-gather.6.cloned.1.call-update
  10.0 2.0 %stack.2 = bf16[32,128,128]{2,1,0:T(8,128)(2,1)} broadcast(bf16[128,128]{1,0:T(8,128)(2,1)} %param.9), dimensions={1,2} | broadcast | bytes 1081344 | tf_op jit(solution)/shard_map/stack | solution.py:55
  12.0 12.0 %all-to-all-start = ((bf16[32,128,128]{2,1,0:T(8,128)(2,1)}), bf16[32,128,128]{2,1,0:T(8,128)(2,1)S(1)}, u32[]{:S(2)}, u32[]{:S(2)}) async-start(bf16[32,128,128]{2,1,0:T(8,128)(2,1)} %stack.2), calls=%async_computation | async-start | bytes 2097152 | tf_op jit(solution)/shard_map/all_to_all | solution.py:55
  24.0 0.0 all-gather.4.cloned.1.call-start
  24.1 1.0 copy.20
  25.2 0.2 multiply_cosine_fusion.1
  25.4 57.9 %all-gather.6.cloned.1.call-done = bf16[4096,1,128]{0,2,1:T(8,128)(2,1)} async-done(((bf16[128,1,128]{0,2,1:T(8,128)(2,1)}), bf16[4096,1,128]{0,2,1:T(8,128)(2,1)}) %all-gather.6.cloned.1.call-update) | async-done | bytes 1048592 | tf_op jit(solution)/shard_map/all_gather | solution.py:53
  83.3 0.0 all-to-all-done
  83.4 7.3 %conditional.1 = (f32[1,4,128]{2,1,0:T(4,128)S(1)}, f32[1,4,128,128]{2,3,1,0:T(8,128)S(1)}) conditional(s32[]{:T(128)} %convert_element_type.42, () %tuple.13, (s32[]{:T(128)}, s32[128]{0:T(128)S(1)}, s32[128]{0:T(128)S(1)}, bf16[128,4,128]{0,2,1:T(8,128)(2,1)S(1)}, bf16[4096,128]{0,1:T(8,128)(2,1)}, ...), branch_computations={%region_2.3_spmd, %region_3.6_spmd} | conditional | flops 1102577280 | bytes 30029844 | solution.py:81
  83.4 0.1 copy.22
  83.5 0.5 fusion.7
  84.0 2.6 %fusion = (f32[4,128]{1,0:T(4,128)S(1)}, f32[4096,128,4]{1,0,2:T(8,128)S(1)}) fusion(pred[128,4096]{0,1:T(8,128)(4,1)S(1)} %fusion.7, bf16[128,4,128]{2,0,1:T(8,128)(2,1)S(1)} %copy.22, bf16[4096,128]{0,1:T(8,128)(2,1)} %get-tuple-element.47), kind=kOutput, calls=%fused_computation.2 | convolution fusion | flops 543161856 | bytes 10094592 | tf_op jit(solution)/shard_map/cond/branch_1_fun/tkgd,nkd->kgtn/dot_general | solution.py:63
  86.6 1.9 %fusion.8 = f32[1,4,128,128]{2,3,1,0:T(8,128)S(1)} fusion(bf16[4096,128,1]{1,0,2:T(8,128)(2,1)S(1)} %bitcast.51, f32[4096,128,4]{1,0,2:T(8,128)S(1)} %get-tuple-element.51, f32[4,128]{1,0:T(4,128)S(1)} %broadcast_maximum_fusion, pred[128,4096]{0,1:T(8,128)(4,1)S(1)} %fusion.7), kind=kOutput, calls=%fused_computation.11 | convolution fusion | flops 547356672 | bytes 10225664 | tf_op jit(solution)/shard_map/cond/branch_1_fun/kgtn,nkd->kgtd/dot_general | solution.py:72
  88.5 2.1 %fusion.2 = f32[4,128]{1,0:T(4,128)S(1)} fusion(f32[4096,128,4]{1,0,2:T(8,128)S(1)} %get-tuple-element.51, f32[4,128]{1,0:T(4,128)S(1)} %broadcast_maximum_fusion, pred[128,4096]{0,1:T(8,128)(4,1)S(1)} %fusion.7), kind=kLoop, calls=%fused_computation.4 | loop fusion | flops 10485248 | bytes 8916992 | tf_op jit(solution)/shard_map/cond/branch_1_fun/reduce_sum | solution.py:71
  90.6 0.7 divide_convert_fusion
  91.3 0.0 all-gather.4.cloned.1.call-update
  91.3 29.4 %all-gather.4.cloned.1.call-done = bf16[128,4096]{0,1:T(8,128)(2,1)} async-done(((bf16[128,512]{0,1:T(8,128)(2,1)}), bf16[128,4096]{0,1:T(8,128)(2,1)}) %all-gather.4.cloned.1.call-update) | async-done | bytes 1048592 | tf_op jit(solution)/shard_map/all_gather | solution.py:86
  120.8 5.7 %convolution_convert_fusion = bf16[128,1024]{1,0:T(8,128)(2,1)} fusion(bf16[128,4096]{0,1:T(8,128)(2,1)} %all-gather.4.cloned.1.call-done, bf16[4096,1024]{1,0:T(8,128)(2,1)} %param.11), kind=kOutput, calls=%fused_computation.20 | convolution fusion | flops 1073872896 | bytes 9699328 | tf_op jit(solution)/shard_map/dot_general | solution.py:85
  (10 shorter events, 0.1 us)
Async XLA Ops:
  6.5 76.8 %all-gather.6.cloned.1.call-start = ((), (), s32[]{:S(2)}) async-start(), calls=%async_computation.2 | async-start | bytes 1081344 | tf_op jit(solution)/shard_map/all_gather | solution.py:53
  12.0 71.4 %all-to-all-start = ((bf16[32,128,128]{2,1,0:T(8,128)(2,1)}), bf16[32,128,128]{2,1,0:T(8,128)(2,1)S(1)}, u32[]{:S(2)}, u32[]{:S(2)}) async-start(bf16[32,128,128]{2,1,0:T(8,128)(2,1)} %stack.2), calls=%async_computation | async-start | bytes 2097152 | tf_op jit(solution)/shard_map/all_to_all | solution.py:55
  24.0 96.7 %all-gather.4.cloned.1.call-start = ((), (), s32[]{:S(2)}) async-start(), calls=%async_computation.1 | async-start | bytes 1179648 | tf_op jit(solution)/shard_map/all_gather | solution.py:86
Sparse Core Ops, SparseCore 0:
  10.1 73.2 all-gather.5
  91.4 29.2 all-gather.3
